TPU v7x, 32 devices: a whole 2x2x4 slice. The times are simulated.
32 devices in a mesh: grp: 2 (over y), tile: 4 (over z), freq: 4 (over x, core).
Axes of the slice: x: 2, y: 2, z: 4, core: 2. Of those that a mesh axis runs over, the one named last changes fastest.
Arguments:
- sources: bfloat16 [4, 4, 2048, 512], P('freq', 'grp', 'tile'), parts along dimension 1, may hold values from -6 to 6
- v_factors: bfloat16 [4, 4, 2, 4, 112, 512], P('freq', 'tile', None, 'grp'), parts along dimension 3, may hold values from -0.1875 to 0.1875
- u_factors: bfloat16 [4, 4, 4, 112, 1024], P('freq', None, 'grp', None, 'tile'), parts along dimension 2, may hold values from -0.1875 to 0.1875
- tile_ranks: int32 [4, 4, 4], P('freq', 'grp', 'tile'), parts along dimension 1, may hold values from 16 to 112, as said below
- window_bounds: int32 [4, 1024, 512], P('grp', ('tile', 'freq')), parts along dimension 0, may hold values from 0 to 31, as said below
Outputs:
- windowed_traces: float32 [1024, 64, 512], P(('tile', 'freq'), 'grp'), parts along dimension 1
There are 2 independent parts, one for each index of `grp`. A program takes and returns all parts, laid end to end along the dimension named above; each array names one. Nothing has to cross between parts.
Inputs may be any that keep to these rules, and one draw needn't show every extreme that they name: `tile_ranks`: each tile's rank for each frequency; rank slots at or beyond it carry no coefficients. window_bounds[1] - window_bounds[0] lies between 8 and 16 for every receiver and virtual source.
All inputs are finite; a program needn't handle non-finite values.
Results may differ from a plain program's by a relative error of at most 0.0041.
Values may be sent and summed in bfloat16 or wider, within the bound.
No kernel may reach another device: no remote copies, remote signals or barrier semaphores. Data moves between devices by JAX's collectives and lax.ppermute only.
A program may use at most 64 MiB of HBM per device.

v0:
```python
import math
import jax
import jax.numpy as jnp
from jax import lax
from jax.sharding import PartitionSpec as P

NT = 32
S_CHUNKS = 2
first_bin = 2


def inverse_tables(count_freq, count_time):
    freq_index = jnp.arange(count_freq, dtype=jnp.int32)[:, None] + first_bin
    time_index = jnp.arange(count_time, dtype=jnp.int32)[None, :]
    phase_step = freq_index * time_index % count_time
    angles = phase_step.astype(jnp.float32) * (2.0 * math.pi / count_time)
    return (jnp.cos(angles), jnp.sin(angles))


def column_products(v_local, x_local, rank_local):
    products = lax.dot_general(
        v_local, x_local, (((3,), (1,)), ((), ())), preferred_element_type=jnp.float32
    )
    coef_real = products[:, 0, :, 0] - products[:, 1, :, 1]
    coef_imag = products[:, 0, :, 1] + products[:, 1, :, 0]
    slot_index = jnp.arange(v_local.shape[2], dtype=jnp.int32)
    live_slots = slot_index[None, :, None] < rank_local[:, None, None]
    coef_real = jnp.where(live_slots, coef_real, jnp.float32(0.0)).astype(jnp.bfloat16)
    coef_imag = jnp.where(live_slots, coef_imag, jnp.float32(0.0)).astype(jnp.bfloat16)
    return jnp.stack([coef_real, coef_imag], axis=1)


def row_spectrum(u_local, blocks):
    products = lax.dot_general(
        u_local, blocks, (((0, 2), (0, 2)), ((), ())), preferred_element_type=jnp.float32
    )
    real_part = products[0, :, 0] - products[1, :, 1]
    imag_part = products[0, :, 1] + products[1, :, 0]
    return jnp.stack([real_part, imag_part], axis=0).astype(jnp.bfloat16)


def relay_exchange(own, u_local):
    t = lax.axis_index("tile")
    up = [(0, 1), (1, 2), (2, 3)]
    down = [(1, 0), (2, 1), (3, 2)]
    up1 = lax.ppermute(own[1], "tile", up)
    down1 = lax.ppermute(own[0], "tile", down)
    up2 = lax.ppermute(jnp.where(t == 0, own[0], up1), "tile", up)
    down2 = lax.ppermute(jnp.where(t == 3, own[1], down1), "tile", down)
    up3 = lax.ppermute(up2, "tile", [(2, 3)])
    down3 = lax.ppermute(down2, "tile", [(1, 0)])
    orders = (
        lambda: (own[0], down1, down2, down3),
        lambda: (up2, own[0], down1, down2),
        lambda: (up2, up1, own[1], down2),
        lambda: (up3, up2, up1, own[1]),
    )
    branches = [
        (lambda order: lambda: row_spectrum(u_local, jnp.stack(order(), axis=0)))(order)
        for order in orders
    ]
    return lax.switch(t, branches)


def gather_exchange(own, u_local, n_tile):
    repeat = n_tile // own.shape[0]
    sending = jnp.repeat(own, repeat, axis=0)
    received = lax.all_to_all(sending, "tile", split_axis=0, concat_axis=0, tiled=True)
    return row_spectrum(u_local, received)


def make_per_device(n_tile):

    def per_device(sources, v_factors, u_factors, tile_ranks, window_bounds):
        v_local = v_factors[0, 0]
        u_local = u_factors[0]
        x_local = sources[0]
        rank_local = tile_ranks[0, :, 0]
        rows = v_local.shape[0]
        use_relay = n_tile == 4 and rows == 2 and (u_local.shape[0] == 4)
        count_s = x_local.shape[2]
        chunks = S_CHUNKS if count_s % S_CHUNKS == 0 else 1
        width = count_s // chunks
        received_parts = []
        for c in range(chunks):
            x_part = x_local[:, :, c * width : (c + 1) * width]
            own = column_products(v_local, x_part, rank_local)
            if use_relay:
                spectrum = relay_exchange(own, u_local)
            else:
                spectrum = gather_exchange(own, u_local, n_tile)
            received_parts.append(
                lax.all_to_all(spectrum[None], "freq", split_axis=2, concat_axis=0, tiled=True)
            )
        received = jnp.concatenate(received_parts, axis=3) if chunks > 1 else received_parts[0]
        count_freq = received.shape[0]
        cosine_table, sine_table = inverse_tables(count_freq, NT)
        widened = received.astype(jnp.float32)
        real_sum = 0.0
        imag_sum = 0.0
        for f in range(count_freq):
            real_sum = real_sum + widened[f, 0][:, None, :] * cosine_table[f][None, :, None]
            imag_sum = imag_sum + widened[f, 1][:, None, :] * sine_table[f][None, :, None]
        traces = (real_sum - imag_sum) * (1.0 / math.sqrt(count_freq))
        time_index = jnp.arange(NT, dtype=jnp.int32)[None, :, None]
        inside = (time_index >= window_bounds[0][:, None, :]) & (
            time_index < window_bounds[1][:, None, :]
        )
        return jnp.where(inside, traces, jnp.float32(0.0))

    return per_device


def solution(mesh):
    return jax.shard_map(
        make_per_device(mesh.shape["tile"]),
        mesh=mesh,
        in_specs=(
            P("freq", "grp", "tile", None),
            P("freq", "tile", None, "grp", None, None),
            P("freq", None, "grp", None, "tile"),
            P("freq", "grp", "tile"),
            P("grp", ("tile", "freq"), None),
        ),
        out_specs=P(("tile", "freq"), "grp", None),
        check_vma=False,
    )
```

profile of v0, /device:TPU:0, one launch (start us, length us, event | category | flops | bytes accessed | tf_op | source)
XLA Modules:
  0.0 69.7 jit_solution(6855587100608741447)
XLA Ops:
  0.0 0.0 copy-start
  0.0 0.0 copy-start.2
  0.0 1.0 %copy-done = bf16[1,1,2,2,112,512]{5,4,3,2,1,0:T(8,128)(2,1)S(1)} copy-done((bf16[1,1,2,2,112,512]{5,4,3,2,1,0:T(8,128)(2,1)S(1)}, bf16[1,1,2,2,112,512]{5,4,3,2,1,0:T(8,128)(2,1)}, u32[]{:S(2)}) %copy-start) | copy-done | bytes 458776
  1.0 0.0 copy-start.1
  1.0 1.5 %fusion.90 = f32[2,2,112,2,256]{4,2,3,1,0:T(8,128)S(1)} fusion(bf16[2,512,512]{2,1,0:T(8,128)(2,1)} %bitcast.377, bf16[1,1,2,2,112,512]{5,4,3,2,1,0:T(8,128)(2,1)S(1)} %copy-done), kind=kOutput, calls=%fused_computation.143 | convolution fusion | flops 234881024 | bytes 1900544 | tf_op jit(solution)/shard_map/dot_general | solution.py:21
  2.5 1.4 %fusion.89 = f32[2,2,112,2,256]{4,2,0,3,1:T(8,128)S(1)} fusion(bf16[2,512,512]{2,1,0:T(8,128)(2,1)} %bitcast.378, bf16[1,1,2,2,112,512]{5,4,3,2,1,0:T(8,128)(2,1)S(1)} %copy-done), kind=kOutput, calls=%fused_computation.141 | convolution fusion | flops 234881024 | bytes 1900544 | tf_op jit(solution)/shard_map/dot_general | solution.py:21
  4.0 0.7 %iota_compare_fusion.2 = pred[2,112]{1,0:T(4,128)(4,1)S(1)} fusion(s32[2]{0:T(128)} %bitcast.408), kind=kLoop, calls=%fused_computation.207 | loop fusion | flops 224 | bytes 232 | tf_op jit(solution)/shard_map/lt | solution.py:27
  4.7 0.1 fusion.101
  4.8 0.1 fusion.98
  5.0 4.9 %collective-permute-start.3 = (bf16[2,112,256]{2,1,0:T(8,128)(2,1)S(1)}, bf16[2,112,256]{2,1,0:T(8,128)(2,1)S(1)}, u32[]{:S(2)}, u32[]{:S(2)}) collective-permute-start(bf16[2,112,256]{2,1,0:T(8,128)(2,1)S(1)} %fusion.114), channel_id=1, source_target_pairs={{0,4},{4,8},{8,12},{1,5},{5,9},{9,13},{2,6},{6,10},{10,14},{3,7},{... | collective-permute-start | bytes 344072 | tf_op jit(solution)/shard_map/ppermute | solution.py:46
  9.9 3.5 %collective-permute-start.9 = (bf16[2,112,256]{2,1,0:T(8,128)(2,1)S(1)}, bf16[2,112,256]{2,1,0:T(8,128)(2,1)S(1)}, u32[]{:S(2)}, u32[]{:S(2)}) collective-permute-start(bf16[2,112,256]{2,1,0:T(8,128)(2,1)S(1)} %fusion.110), channel_id=1, source_target_pairs={{0,4},{4,8},{8,12},{1,5},{5,9},{9,13},{2,6},{6,10},{10,14},{3,7},{... | collective-permute-start | bytes 344072 | tf_op jit(solution)/shard_map/ppermute | solution.py:46
  13.4 0.0 copy-done.2
  13.5 2.3 %collective-permute-done.9 = bf16[2,112,256]{2,1,0:T(8,128)(2,1)S(1)} collective-permute-done((bf16[2,112,256]{2,1,0:T(8,128)(2,1)S(1)}, bf16[2,112,256]{2,1,0:T(8,128)(2,1)S(1)}, u32[]{:S(2)}, u32[]{:S(2)}) %collective-permute-start.9) | collective-permute-done | bytes 114720 | tf_op jit(solution)/shard_map/ppermute | solution.py:46
  15.8 5.0 %collective-permute-start.10 = (bf16[2,112,256]{2,1,0:T(8,128)(2,1)S(1)}, bf16[2,112,256]{2,1,0:T(8,128)(2,1)}, u32[]{:S(2)}, u32[]{:S(2)}) collective-permute-start(bf16[2,112,256]{2,1,0:T(8,128)(2,1)S(1)} %get-tuple-element.201), channel_id=1, source_target_pairs={{0,4},{4,8},{8,12},{1,5},{5,9},{9,13},{2,6},{6,10},{10,14},{3,7},{... | collective-permute-start | bytes 344072 | tf_op jit(solution)/shard_map/ppermute | solution.py:48
  20.8 1.3 %collective-permute-start.6 = (bf16[2,112,256]{2,1,0:T(8,128)(2,1)S(1)}, bf16[2,112,256]{2,1,0:T(8,128)(2,1)S(1)}, u32[]{:S(2)}, u32[]{:S(2)}) collective-permute-start(bf16[2,112,256]{2,1,0:T(8,128)(2,1)S(1)} %get-tuple-element.202), channel_id=1, source_target_pairs={{4,0},{8,4},{12,8},{5,1},{9,5},{13,9},{6,2},{10,6},{14,10},{7,3},{... | collective-permute-start | bytes 344072 | tf_op jit(solution)/shard_map/ppermute | solution.py:47
  22.1 0.0 collective-permute-done.3
  22.1 1.3 %collective-permute-start = (bf16[2,112,256]{2,1,0:T(8,128)(2,1)S(1)}, bf16[2,112,256]{2,1,0:T(8,128)(2,1)S(1)}, u32[]{:S(2)}, u32[]{:S(2)}) collective-permute-start(bf16[2,112,256]{2,1,0:T(8,128)(2,1)S(1)} %get-tuple-element.200), channel_id=1, source_target_pairs={{4,0},{8,4},{12,8},{5,1},{9,5},{13,9},{6,2},{10,6},{14,10},{7,3},{... | collective-permute-start | bytes 344072 | tf_op jit(solution)/shard_map/ppermute | solution.py:47
  23.4 4.4 %collective-permute-done.6 = bf16[2,112,256]{2,1,0:T(8,128)(2,1)S(1)} collective-permute-done((bf16[2,112,256]{2,1,0:T(8,128)(2,1)S(1)}, bf16[2,112,256]{2,1,0:T(8,128)(2,1)S(1)}, u32[]{:S(2)}, u32[]{:S(2)}) %collective-permute-start.6) | collective-permute-done | bytes 114720 | tf_op jit(solution)/shard_map/ppermute | solution.py:47
  27.8 1.3 %collective-permute-start.7 = (bf16[2,112,256]{2,1,0:T(8,128)(2,1)S(1)}, bf16[2,112,256]{2,1,0:T(8,128)(2,1)S(1)}, u32[]{:S(2)}, u32[]{:S(2)}) collective-permute-start(bf16[2,112,256]{2,1,0:T(8,128)(2,1)S(1)} %broadcast_select_fusion.2), channel_id=1, source_target_pairs={{4,0},{8,4},{12,8},{5,1},{9,5},{13,9},{6,2},{10,6},{14,10},{7,3},{... | collective-permute-start | bytes 344072 | tf_op jit(solution)/shard_map/ppermute | solution.py:49
  29.1 0.0 copy-done.1
  29.2 4.6 %collective-permute-start.4 = (bf16[2,112,256]{2,1,0:T(8,128)(2,1)S(1)}, bf16[2,112,256]{2,1,0:T(8,128)(2,1)S(1)}, u32[]{:S(2)}, u32[]{:S(2)}) collective-permute-start(bf16[2,112,256]{2,1,0:T(8,128)(2,1)S(1)} %get-tuple-element.199), channel_id=1, source_target_pairs={{0,4},{4,8},{8,12},{1,5},{5,9},{9,13},{2,6},{6,10},{10,14},{3,7},{... | collective-permute-start | bytes 344072 | tf_op jit(solution)/shard_map/ppermute | solution.py:48
  33.8 0.0 collective-permute-done.10
  33.8 0.7 collective-permute-start.11
  34.5 0.0 collective-permute-done.7
  34.5 1.3 %collective-permute-start.8 = (bf16[2,112,256]{2,1,0:T(8,128)(2,1)S(1)}, bf16[2,112,256]{2,1,0:T(8,128)(2,1)S(1)}, u32[]{:S(2)}, u32[]{:S(2)}) collective-permute-start(bf16[2,112,256]{2,1,0:T(8,128)(2,1)S(1)} %collective-permute-done.7), channel_id=1, source_target_pairs={{4,0},{5,1},{6,2},{7,3},{20,16},{21,17},{22,18},{23,19}} | collective-permute-start | bytes 344072 | tf_op jit(solution)/shard_map/ppermute | solution.py:51
  35.8 0.0 collective-permute-done
  35.8 1.3 %collective-permute-start.1 = (bf16[2,112,256]{2,1,0:T(8,128)(2,1)S(1)}, bf16[2,112,256]{2,1,0:T(8,128)(2,1)S(1)}, u32[]{:S(2)}, u32[]{:S(2)}) collective-permute-start(bf16[2,112,256]{2,1,0:T(8,128)(2,1)S(1)} %broadcast_select_fusion.3), channel_id=1, source_target_pairs={{4,0},{8,4},{12,8},{5,1},{9,5},{13,9},{6,2},{10,6},{14,10},{7,3},{... | collective-permute-start | bytes 344072 | tf_op jit(solution)/shard_map/ppermute | solution.py:49
  37.1 0.0 collective-permute-done.11
  37.1 4.0 %collective-permute-done.8 = bf16[2,112,256]{2,1,0:T(8,128)(2,1)S(1)} collective-permute-done((bf16[2,112,256]{2,1,0:T(8,128)(2,1)S(1)}, bf16[2,112,256]{2,1,0:T(8,128)(2,1)S(1)}, u32[]{:S(2)}, u32[]{:S(2)}) %collective-permute-start.8) | collective-permute-done | bytes 114720 | tf_op jit(solution)/shard_map/ppermute | solution.py:51
  41.2 0.6 conditional.5
  41.2 0.5 convolution_bitcast_fusion.4
  41.8 0.9 %copy.148 = bf16[2,256,256]{2,0,1:T(2,128)(2,1)} copy(bf16[2,256,256]{1,2,0:T(8,128)(2,1)S(1)} %get-tuple-element.231) | data formatting | bytes 524288
  42.7 3.4 %all-to-all-start.1 = ((bf16[1,2,256,256]{3,1,0,2:T(2,128)(2,1)}), bf16[1,2,256,256]{3,1,0,2:T(2,128)(2,1)S(1)}, u32[]{:S(2)}, u32[]{:S(2)}) async-start(bf16[1,2,256,256]{3,1,0,2:T(2,128)(2,1)} %bitcast.124), calls=%async_computation.1 | async-start | bytes 524288 | tf_op jit(solution)/shard_map/all_to_all | solution.py:93
  46.1 0.1 fusion.119
  46.2 0.0 collective-permute-done.4
  46.2 0.7 collective-permute-start.5
  46.9 0.0 collective-permute-done.1
  46.9 1.3 %collective-permute-start.2 = (bf16[2,112,256]{2,1,0:T(8,128)(2,1)S(1)}, bf16[2,112,256]{2,1,0:T(8,128)(2,1)S(1)}, u32[]{:S(2)}, u32[]{:S(2)}) collective-permute-start(bf16[2,112,256]{2,1,0:T(8,128)(2,1)S(1)} %collective-permute-done.1), channel_id=1, source_target_pairs={{4,0},{5,1},{6,2},{7,3},{20,16},{21,17},{22,18},{23,19}} | collective-permute-start | bytes 344072 | tf_op jit(solution)/shard_map/ppermute | solution.py:51
  48.2 0.0 collective-permute-done.5
  48.2 6.1 %collective-permute-done.2 = bf16[2,112,256]{2,1,0:T(8,128)(2,1)S(1)} collective-permute-done((bf16[2,112,256]{2,1,0:T(8,128)(2,1)S(1)}, bf16[2,112,256]{2,1,0:T(8,128)(2,1)S(1)}, u32[]{:S(2)}, u32[]{:S(2)}) %collective-permute-start.2) | collective-permute-done | bytes 114720 | tf_op jit(solution)/shard_map/ppermute | solution.py:51
  54.3 0.6 conditional.4
  54.3 0.5 convolution_bitcast_fusion
  54.9 0.9 %copy.147 = bf16[2,256,256]{2,0,1:T(2,128)(2,1)} copy(bf16[2,256,256]{1,2,0:T(8,128)(2,1)S(1)} %get-tuple-element.230) | data formatting | bytes 524288
  55.8 0.0 all-to-all-done.1
  55.8 3.4 %all-to-all-start = ((bf16[1,2,256,256]{3,1,0,2:T(2,128)(2,1)}), bf16[1,2,256,256]{3,1,0,2:T(2,128)(2,1)S(1)}, u32[]{:S(2)}, u32[]{:S(2)}) async-start(bf16[1,2,256,256]{3,1,0,2:T(2,128)(2,1)} %bitcast.113), calls=%async_computation | async-start | bytes 524288 | tf_op jit(solution)/shard_map/all_to_all | solution.py:93
  59.2 5.9 %all-to-all-done = bf16[1,2,256,256]{3,1,0,2:T(2,128)(2,1)S(1)} async-done(((bf16[1,2,256,256]{3,1,0,2:T(2,128)(2,1)}), bf16[1,2,256,256]{3,1,0,2:T(2,128)(2,1)S(1)}, u32[]{:S(2)}, u32[]{:S(2)}) %all-to-all-start) | async-done | bytes 262176 | tf_op jit(solution)/shard_map/all_to_all | solution.py:93
  65.2 0.1 maximum_convert_fusion
  65.3 0.1 slice_bitcast_fusion.29
  65.4 4.3 %multiply_select_fusion = f32[64,32,512]{2,1,0:T(8,128)} fusion(f32[32]{0:T(128)S(1)} %get-tuple-element.220, f32[64,512]{1,0:T(8,128)S(1)} %get-tuple-element.204, f32[32]{0:T(128)S(1)} %get-tuple-element.221, f32[64,512]{1,0:T(8,128)S(1)} %get-tuple-element.205, f32[32]{0:T(128)S(1)} %get-tuple-element.222, f32[64,512]{1,0:T(8,128)S(1)} %get-tuple-element.206, ...), kind=kLoop, calls=%fused_computation.136 | loop fusion | flops 20971520 | bytes 5506048 | tf_op jit(solution)/shard_map/jit(_where)/select_n | solution.py:109
  (23 shorter events, 0.5 us)
Async XLA Ops:
  0.0 1.0 %copy-start = (bf16[1,1,2,2,112,512]{5,4,3,2,1,0:T(8,128)(2,1)S(1)}, bf16[1,1,2,2,112,512]{5,4,3,2,1,0:T(8,128)(2,1)}, u32[]{:S(2)}) copy-start(bf16[1,1,2,2,112,512]{5,4,3,2,1,0:T(8,128)(2,1)} %param.14) | copy-start | bytes 1376260
  0.0 13.4 %copy-start.2 = (s32[2,64,512]{2,1,0:T(8,128)S(1)}, s32[2,64,512]{2,1,0:T(8,128)}, u32[]{:S(2)}) copy-start(s32[2,64,512]{2,1,0:T(8,128)} %param.17) | copy-start | bytes 786436
  1.0 28.1 %copy-start.1 = (bf16[1,4,2,112,256]{4,3,2,1,0:T(8,128)(2,1)S(1)}, bf16[1,4,2,112,256]{4,3,2,1,0:T(8,128)(2,1)}, u32[]{:S(2)}) copy-start(bf16[1,4,2,112,256]{4,3,2,1,0:T(8,128)(2,1)} %param.15) | copy-start | bytes 1376260
  5.0 17.1 %collective-permute-start.3 = (bf16[2,112,256]{2,1,0:T(8,128)(2,1)S(1)}, bf16[2,112,256]{2,1,0:T(8,128)(2,1)S(1)}, u32[]{:S(2)}, u32[]{:S(2)}) collective-permute-start(bf16[2,112,256]{2,1,0:T(8,128)(2,1)S(1)} %fusion.114), channel_id=1, source_target_pairs={{0,4},{4,8},{8,12},{1,5},{5,9},{9,13},{2,6},{6,10},{10,14},{3,7},{... | collective-permute-start | bytes 344072 | tf_op jit(solution)/shard_map/ppermute | solution.py:46
  9.9 5.8 %collective-permute-start.9 = (bf16[2,112,256]{2,1,0:T(8,128)(2,1)S(1)}, bf16[2,112,256]{2,1,0:T(8,128)(2,1)S(1)}, u32[]{:S(2)}, u32[]{:S(2)}) collective-permute-start(bf16[2,112,256]{2,1,0:T(8,128)(2,1)S(1)} %fusion.110), channel_id=1, source_target_pairs={{0,4},{4,8},{8,12},{1,5},{5,9},{9,13},{2,6},{6,10},{10,14},{3,7},{... | collective-permute-start | bytes 344072 | tf_op jit(solution)/shard_map/ppermute | solution.py:46
  15.8 18.0 %collective-permute-start.10 = (bf16[2,112,256]{2,1,0:T(8,128)(2,1)S(1)}, bf16[2,112,256]{2,1,0:T(8,128)(2,1)}, u32[]{:S(2)}, u32[]{:S(2)}) collective-permute-start(bf16[2,112,256]{2,1,0:T(8,128)(2,1)S(1)} %get-tuple-element.201), channel_id=1, source_target_pairs={{0,4},{4,8},{8,12},{1,5},{5,9},{9,13},{2,6},{6,10},{10,14},{3,7},{... | collective-permute-start | bytes 344072 | tf_op jit(solution)/shard_map/ppermute | solution.py:48
  20.8 7.0 %collective-permute-start.6 = (bf16[2,112,256]{2,1,0:T(8,128)(2,1)S(1)}, bf16[2,112,256]{2,1,0:T(8,128)(2,1)S(1)}, u32[]{:S(2)}, u32[]{:S(2)}) collective-permute-start(bf16[2,112,256]{2,1,0:T(8,128)(2,1)S(1)} %get-tuple-element.202), channel_id=1, source_target_pairs={{4,0},{8,4},{12,8},{5,1},{9,5},{13,9},{6,2},{10,6},{14,10},{7,3},{... | collective-permute-start | bytes 344072 | tf_op jit(solution)/shard_map/ppermute | solution.py:47
  22.1 13.7 %collective-permute-start = (bf16[2,112,256]{2,1,0:T(8,128)(2,1)S(1)}, bf16[2,112,256]{2,1,0:T(8,128)(2,1)S(1)}, u32[]{:S(2)}, u32[]{:S(2)}) collective-permute-start(bf16[2,112,256]{2,1,0:T(8,128)(2,1)S(1)} %get-tuple-element.200), channel_id=1, source_target_pairs={{4,0},{8,4},{12,8},{5,1},{9,5},{13,9},{6,2},{10,6},{14,10},{7,3},{... | collective-permute-start | bytes 344072 | tf_op jit(solution)/shard_map/ppermute | solution.py:47
  27.8 6.7 %collective-permute-start.7 = (bf16[2,112,256]{2,1,0:T(8,128)(2,1)S(1)}, bf16[2,112,256]{2,1,0:T(8,128)(2,1)S(1)}, u32[]{:S(2)}, u32[]{:S(2)}) collective-permute-start(bf16[2,112,256]{2,1,0:T(8,128)(2,1)S(1)} %broadcast_select_fusion.2), channel_id=1, source_target_pairs={{4,0},{8,4},{12,8},{5,1},{9,5},{13,9},{6,2},{10,6},{14,10},{7,3},{... | collective-permute-start | bytes 344072 | tf_op jit(solution)/shard_map/ppermute | solution.py:49
  29.2 17.0 %collective-permute-start.4 = (bf16[2,112,256]{2,1,0:T(8,128)(2,1)S(1)}, bf16[2,112,256]{2,1,0:T(8,128)(2,1)S(1)}, u32[]{:S(2)}, u32[]{:S(2)}) collective-permute-start(bf16[2,112,256]{2,1,0:T(8,128)(2,1)S(1)} %get-tuple-element.199), channel_id=1, source_target_pairs={{0,4},{4,8},{8,12},{1,5},{5,9},{9,13},{2,6},{6,10},{10,14},{3,7},{... | collective-permute-start | bytes 344072 | tf_op jit(solution)/shard_map/ppermute | solution.py:48
  33.8 3.3 %collective-permute-start.11 = (bf16[2,112,256]{2,1,0:T(8,128)(2,1)}, bf16[2,112,256]{2,1,0:T(8,128)(2,1)S(1)}, u32[]{:S(2)}, u32[]{:S(2)}) collective-permute-start(bf16[2,112,256]{2,1,0:T(8,128)(2,1)} %collective-permute-done.10), channel_id=1, source_target_pairs={{8,12},{9,13},{10,14},{11,15},{24,28},{25,29},{26,30},{27,31}} | collective-permute-start | bytes 344072 | tf_op jit(solution)/shard_map/ppermute | solution.py:50
  34.5 6.7 %collective-permute-start.8 = (bf16[2,112,256]{2,1,0:T(8,128)(2,1)S(1)}, bf16[2,112,256]{2,1,0:T(8,128)(2,1)S(1)}, u32[]{:S(2)}, u32[]{:S(2)}) collective-permute-start(bf16[2,112,256]{2,1,0:T(8,128)(2,1)S(1)} %collective-permute-done.7), channel_id=1, source_target_pairs={{4,0},{5,1},{6,2},{7,3},{20,16},{21,17},{22,18},{23,19}} | collective-permute-start | bytes 344072 | tf_op jit(solution)/shard_map/ppermute | solution.py:51
  35.8 11.1 %collective-permute-start.1 = (bf16[2,112,256]{2,1,0:T(8,128)(2,1)S(1)}, bf16[2,112,256]{2,1,0:T(8,128)(2,1)S(1)}, u32[]{:S(2)}, u32[]{:S(2)}) collective-permute-start(bf16[2,112,256]{2,1,0:T(8,128)(2,1)S(1)} %broadcast_select_fusion.3), channel_id=1, source_target_pairs={{4,0},{8,4},{12,8},{5,1},{9,5},{13,9},{6,2},{10,6},{14,10},{7,3},{... | collective-permute-start | bytes 344072 | tf_op jit(solution)/shard_map/ppermute | solution.py:49
  42.7 13.1 %all-to-all-start.1 = ((bf16[1,2,256,256]{3,1,0,2:T(2,128)(2,1)}), bf16[1,2,256,256]{3,1,0,2:T(2,128)(2,1)S(1)}, u32[]{:S(2)}, u32[]{:S(2)}) async-start(bf16[1,2,256,256]{3,1,0,2:T(2,128)(2,1)} %bitcast.124), calls=%async_computation.1 | async-start | bytes 524288 | tf_op jit(solution)/shard_map/all_to_all | solution.py:93
  46.2 2.0 %collective-permute-start.5 = (bf16[2,112,256]{2,1,0:T(8,128)(2,1)S(1)}, bf16[2,112,256]{2,1,0:T(8,128)(2,1)S(1)}, u32[]{:S(2)}, u32[]{:S(2)}) collective-permute-start(bf16[2,112,256]{2,1,0:T(8,128)(2,1)S(1)} %collective-permute-done.4), channel_id=1, source_target_pairs={{8,12},{9,13},{10,14},{11,15},{24,28},{25,29},{26,30},{27,31}} | collective-permute-start | bytes 344072 | tf_op jit(solution)/shard_map/ppermute | solution.py:50
  46.9 7.4 %collective-permute-start.2 = (bf16[2,112,256]{2,1,0:T(8,128)(2,1)S(1)}, bf16[2,112,256]{2,1,0:T(8,128)(2,1)S(1)}, u32[]{:S(2)}, u32[]{:S(2)}) collective-permute-start(bf16[2,112,256]{2,1,0:T(8,128)(2,1)S(1)} %collective-permute-done.1), channel_id=1, source_target_pairs={{4,0},{5,1},{6,2},{7,3},{20,16},{21,17},{22,18},{23,19}} | collective-permute-start | bytes 344072 | tf_op jit(solution)/shard_map/ppermute | solution.py:51
  55.8 9.4 %all-to-all-start = ((bf16[1,2,256,256]{3,1,0,2:T(2,128)(2,1)}), bf16[1,2,256,256]{3,1,0,2:T(2,128)(2,1)S(1)}, u32[]{:S(2)}, u32[]{:S(2)}) async-start(bf16[1,2,256,256]{3,1,0,2:T(2,128)(2,1)} %bitcast.113), calls=%async_computation | async-start | bytes 524288 | tf_op jit(solution)/shard_map/all_to_all | solution.py:93
where the time goes:
time: 70.3 us; the launch traced here: 69.7 us
  starting transfers between devices  33.8 us (48%)
  waiting for transfers between devices  22.8 us (32%)
  other arithmetic  5.77 us (8%)
  matrix products  3.87 us (6%)
  local copies, waits for them, and re-layouts  2.97 us (4%)
    ppermute x2, waiting for transfers between devices, relay_exchange(): down3 = lax.ppermute(down2, 'tile', [(1, 0)])  10.1 us
    ppermute x2, starting transfers between devices, relay_exchange(): up2 = lax.ppermute(jnp.where(t == 0, own[0], up1), 'tile', up)  9.53 us
    ppermute x2, starting transfers between devices, relay_exchange(): up1 = lax.ppermute(own[1], 'tile', up)  8.42 us
    all_to_all x2, starting transfers between devices, per_device(): lax.all_to_all(spectrum[None], 'freq', split_axis=2, concat_axis=0, tiled...  6.81 us
    all_to_all x2, waiting for transfers between devices, per_device(): lax.all_to_all(spectrum[None], 'freq', split_axis=2, concat_axis=0, tiled...  5.95 us
    ppermute x2, waiting for transfers between devices, relay_exchange(): down1 = lax.ppermute(own[0], 'tile', down)  4.4 us
    select_n x1, other arithmetic, per_device(): return jnp.where(inside, traces, jnp.float32(0.0))  4.26 us
    dot_general x2, matrix products, column_products(): lax.dot_general(v_local, x_local, (((3,), (1,)), ((), ())), preferred_ele...  2.94 us
  transfers between devices with their start and end apart: 14, of which 5 were waited for; matrix products, arithmetic and copies ran while one was open for 5% of the time, Pallas kernels for 0%

commit v1 on v0

--- a/solution.py
+++ b/solution.py
@@ -7,6 +7,20 @@
 NT = 32
 S_CHUNKS = 2
 first_bin = 2
+
+
+def refer_the_digits(my_tile, dim_k, work_x):
+    row_out = my_tile.shape
+    t_next = my_tile.reshape(
+        *row_out[:dim_k], work_x, row_out[dim_k] // work_x, *row_out[dim_k + 1 :]
+    )
+    return jnp.moveaxis(t_next, dim_k, 0)
+
+
+def _bind_page(message, d_out):
+    s_next = list(message.shape[1:])
+    s_next[d_out] *= message.shape[0]
+    return jnp.moveaxis(message, 0, d_out).reshape(s_next)
 
 
 def inverse_tables(count_freq, count_time):
@@ -89,9 +103,21 @@
                 spectrum = relay_exchange(own, u_local)
             else:
                 spectrum = gather_exchange(own, u_local, n_tile)
-            received_parts.append(
-                lax.all_to_all(spectrum[None], "freq", split_axis=2, concat_axis=0, tiled=True)
-            )
+
+            def update_the_samples(obj, axis_name, v0, view):
+                v1, current_value = (lax.axis_size(axis_name), lax.axis_index(axis_name))
+                next_value = refer_the_digits(obj, v0, v1)
+                new = next_value
+                for h in range(1, v1):
+                    r_now, val = ((current_value + h) % v1, (current_value - h) % v1)
+                    base_arr = lax.dynamic_index_in_dim(next_value, r_now, 0)
+                    k_now = lax.ppermute(
+                        base_arr, axis_name, [(it, (it + h) % v1) for it in range(v1)]
+                    )
+                    new = lax.dynamic_update_slice_in_dim(new, k_now, val, axis=0)
+                return _bind_page(new, view)
+
+            received_parts.append(update_the_samples(spectrum[None], "freq", 2, 0))
         received = jnp.concatenate(received_parts, axis=3) if chunks > 1 else received_parts[0]
         count_freq = received.shape[0]
         cosine_table, sine_table = inverse_tables(count_freq, NT)

time: 70.3 us -> 58 us (0.83)
  waiting for transfers between devices: 22.8 us -> 16.2 us
  starting transfers between devices: 33.8 us -> 29.8 us
  local copies, waits for them, and re-layouts: 2.97 us -> 1.3 us
    ppermute x2, waiting for transfers between devices: 10.1 us -> 2.9 us  [relay_exchange(): down3 = lax.ppermute(down2, 'tile', [(1, 0)])]
    all_to_all x2 -> x0, starting transfers between devices: 6.81 us -> none  [per_device(): lax.all_to_all(spectrum[None], 'freq', split_axis=2, concat_axis=0, tiled...]
    all_to_all x2 -> x0, waiting for transfers between devices: 5.95 us -> none  [per_device(): lax.all_to_all(spectrum[None], 'freq', split_axis=2, concat_axis=0, tiled...]
    ppermute x0 -> x6, waiting for transfers between devices: none -> 4.61 us  [update_the_samples(): lax.ppermute(base_arr, axis_name, [(it, (it + h) % v1) for it in range(v1)])]
    ppermute x0 -> x6, starting transfers between devices: none -> 3.4 us  [update_the_samples(): lax.ppermute(base_arr, axis_name, [(it, (it + h) % v1) for it in range(v1)])]
    ppermute x2, waiting for transfers between devices: 0.04 us -> 2.69 us  [relay_exchange(): down2 = lax.ppermute(jnp.where(t == 3, own[1], down1), 'tile', down)]
    unnamed x9 -> x7, local copies, waits for them, and re-layouts: 2.78 us -> 1.05 us
  transfers between devices with their start and end apart: 14 -> 18, of which waited for: 5 -> 8; matrix products, arithmetic and copies ran while one was open for 5% -> 3% of each run, Pallas kernels for 0% -> 0%
where the time goes in v1:
time: 58 us; the launch traced here: 57.5 us
  starting transfers between devices  29.8 us (51%)
  waiting for transfers between devices  16.2 us (28%)
  other arithmetic  5.76 us (10%)
  matrix products  3.85 us (7%)
  local copies, waits for them, and re-layouts  1.3 us (2%)
    ppermute x2, starting transfers between devices, relay_exchange(): up2 = lax.ppermute(jnp.where(t == 0, own[0], up1), 'tile', up)  8.89 us
    ppermute x2, starting transfers between devices, relay_exchange(): up1 = lax.ppermute(own[1], 'tile', up)  8.42 us
    ppermute x6, waiting for transfers between devices, update_the_samples(): lax.ppermute(base_arr, axis_name, [(it, (it + h) % v1) for it in range(v1)])  4.61 us
    select_n x1, other arithmetic, per_device(): return jnp.where(inside, traces, jnp.float32(0.0))  4.26 us
    ppermute x2, waiting for transfers between devices, relay_exchange(): down1 = lax.ppermute(own[0], 'tile', down)  4.05 us
    ppermute x6, starting transfers between devices, update_the_samples(): lax.ppermute(base_arr, axis_name, [(it, (it + h) % v1) for it in range(v1)])  3.4 us
    ppermute x2, waiting for transfers between devices, relay_exchange(): down3 = lax.ppermute(down2, 'tile', [(1, 0)])  2.9 us
    dot_general x2, matrix products, column_products(): lax.dot_general(v_local, x_local, (((3,), (1,)), ((), ())), preferred_ele...  2.88 us
  transfers between devices with their start and end apart: 18, of which 8 were waited for; matrix products, arithmetic and copies ran while one was open for 3% of the time, Pallas kernels for 0%

profile of v1, /device:TPU:0, one launch (start us, length us, event | category | flops | bytes accessed | tf_op | source)
XLA Modules:
  0.0 57.5 jit_solution(9493087892814764330)
XLA Ops:
  0.0 0.0 copy-start
  0.0 0.0 copy-start.2
  0.0 0.0 copy-start.1
  0.0 1.0 %copy-done = bf16[1,1,2,2,112,512]{5,4,3,2,1,0:T(8,128)(2,1)S(1)} copy-done((bf16[1,1,2,2,112,512]{5,4,3,2,1,0:T(8,128)(2,1)S(1)}, bf16[1,1,2,2,112,512]{5,4,3,2,1,0:T(8,128)(2,1)}, u32[]{:S(2)}) %copy-start) | copy-done | bytes 458776
  1.0 1.4 %fusion.66 = f32[2,2,112,2,256]{4,2,3,1,0:T(8,128)S(1)} fusion(bf16[2,512,512]{2,1,0:T(8,128)(2,1)} %bitcast.299, bf16[1,1,2,2,112,512]{5,4,3,2,1,0:T(8,128)(2,1)S(1)} %copy-done), kind=kOutput, calls=%fused_computation.111 | convolution fusion | flops 234881024 | bytes 1900544 | tf_op jit(solution)/shard_map/dot_general | solution.py:35
  2.5 1.4 %fusion.65 = f32[2,2,112,2,256]{4,2,0,3,1:T(8,128)S(1)} fusion(bf16[2,512,512]{2,1,0:T(8,128)(2,1)} %bitcast.300, bf16[1,1,2,2,112,512]{5,4,3,2,1,0:T(8,128)(2,1)S(1)} %copy-done), kind=kOutput, calls=%fused_computation.109 | convolution fusion | flops 234881024 | bytes 1900544 | tf_op jit(solution)/shard_map/dot_general | solution.py:35
  3.9 0.7 %iota_compare_fusion.2 = pred[2,112]{1,0:T(4,128)(4,1)S(1)} fusion(s32[2]{0:T(128)} %bitcast.349), kind=kLoop, calls=%fused_computation.187 | loop fusion | flops 224 | bytes 232 | tf_op jit(solution)/shard_map/lt | solution.py:41
  4.6 0.1 fusion.77
  4.7 0.1 fusion.74
  4.9 4.9 %collective-permute-start.3 = (bf16[2,112,256]{2,1,0:T(8,128)(2,1)S(1)}, bf16[2,112,256]{2,1,0:T(8,128)(2,1)S(1)}, u32[]{:S(2)}, u32[]{:S(2)}) collective-permute-start(bf16[2,112,256]{2,1,0:T(8,128)(2,1)S(1)} %fusion.90), channel_id=1, source_target_pairs={{0,4},{4,8},{8,12},{1,5},{5,9},{9,13},{2,6},{6,10},{10,14},{3,7},{... | collective-permute-start | bytes 344072 | tf_op jit(solution)/shard_map/ppermute | solution.py:60
  9.9 3.5 %collective-permute-start.12 = (bf16[2,112,256]{2,1,0:T(8,128)(2,1)S(1)}, bf16[2,112,256]{2,1,0:T(8,128)(2,1)S(1)}, u32[]{:S(2)}, u32[]{:S(2)}) collective-permute-start(bf16[2,112,256]{2,1,0:T(8,128)(2,1)S(1)} %fusion.86), channel_id=1, source_target_pairs={{0,4},{4,8},{8,12},{1,5},{5,9},{9,13},{2,6},{6,10},{10,14},{3,7},{... | collective-permute-start | bytes 344072 | tf_op jit(solution)/shard_map/ppermute | solution.py:60
  13.5 0.1 fusion.95
  13.6 0.0 copy-done.2
  13.6 0.0 copy-done.1
  13.8 1.9 %collective-permute-done.12 = bf16[2,112,256]{2,1,0:T(8,128)(2,1)S(1)} collective-permute-done((bf16[2,112,256]{2,1,0:T(8,128)(2,1)S(1)}, bf16[2,112,256]{2,1,0:T(8,128)(2,1)S(1)}, u32[]{:S(2)}, u32[]{:S(2)}) %collective-permute-start.12) | collective-permute-done | bytes 114720 | tf_op jit(solution)/shard_map/ppermute | solution.py:60
  15.7 4.3 %collective-permute-start.13 = (bf16[2,112,256]{2,1,0:T(8,128)(2,1)S(1)}, bf16[2,112,256]{2,1,0:T(8,128)(2,1)S(1)}, u32[]{:S(2)}, u32[]{:S(2)}) collective-permute-start(bf16[2,112,256]{2,1,0:T(8,128)(2,1)S(1)} %get-tuple-element.169), channel_id=1, source_target_pairs={{0,4},{4,8},{8,12},{1,5},{5,9},{9,13},{2,6},{6,10},{10,14},{3,7},{... | collective-permute-start | bytes 344072 | tf_op jit(solution)/shard_map/ppermute | solution.py:62
  20.1 1.3 %collective-permute-start.9 = (bf16[2,112,256]{2,1,0:T(8,128)(2,1)S(1)}, bf16[2,112,256]{2,1,0:T(8,128)(2,1)S(1)}, u32[]{:S(2)}, u32[]{:S(2)}) collective-permute-start(bf16[2,112,256]{2,1,0:T(8,128)(2,1)S(1)} %get-tuple-element.170), channel_id=1, source_target_pairs={{4,0},{8,4},{12,8},{5,1},{9,5},{13,9},{6,2},{10,6},{14,10},{7,3},{... | collective-permute-start | bytes 344072 | tf_op jit(solution)/shard_map/ppermute | solution.py:61
  21.4 0.0 collective-permute-done.3
  21.4 4.6 %collective-permute-start.4 = (bf16[2,112,256]{2,1,0:T(8,128)(2,1)S(1)}, bf16[2,112,256]{2,1,0:T(8,128)(2,1)S(1)}, u32[]{:S(2)}, u32[]{:S(2)}) collective-permute-start(bf16[2,112,256]{2,1,0:T(8,128)(2,1)S(1)} %get-tuple-element.167), channel_id=1, source_target_pairs={{0,4},{4,8},{8,12},{1,5},{5,9},{9,13},{2,6},{6,10},{10,14},{3,7},{... | collective-permute-start | bytes 344072 | tf_op jit(solution)/shard_map/ppermute | solution.py:62
  26.0 1.3 %collective-permute-start = (bf16[2,112,256]{2,1,0:T(8,128)(2,1)S(1)}, bf16[2,112,256]{2,1,0:T(8,128)(2,1)S(1)}, u32[]{:S(2)}, u32[]{:S(2)}) collective-permute-start(bf16[2,112,256]{2,1,0:T(8,128)(2,1)S(1)} %get-tuple-element.168), channel_id=1, source_target_pairs={{4,0},{8,4},{12,8},{5,1},{9,5},{13,9},{6,2},{10,6},{14,10},{7,3},{... | collective-permute-start | bytes 344072 | tf_op jit(solution)/shard_map/ppermute | solution.py:61
  27.3 0.0 collective-permute-done.9
  27.3 1.3 %collective-permute-start.10 = (bf16[2,112,256]{2,1,0:T(8,128)(2,1)S(1)}, bf16[2,112,256]{2,1,0:T(8,128)(2,1)S(1)}, u32[]{:S(2)}, u32[]{:S(2)}) collective-permute-start(bf16[2,112,256]{2,1,0:T(8,128)(2,1)S(1)} %broadcast_select_fusion.2), channel_id=1, source_target_pairs={{4,0},{8,4},{12,8},{5,1},{9,5},{13,9},{6,2},{10,6},{14,10},{7,3},{... | collective-permute-start | bytes 344072 | tf_op jit(solution)/shard_map/ppermute | solution.py:63
  28.6 4.1 %collective-permute-done = bf16[2,112,256]{2,1,0:T(8,128)(2,1)S(1)} collective-permute-done((bf16[2,112,256]{2,1,0:T(8,128)(2,1)S(1)}, bf16[2,112,256]{2,1,0:T(8,128)(2,1)S(1)}, u32[]{:S(2)}, u32[]{:S(2)}) %collective-permute-start) | collective-permute-done | bytes 114720 | tf_op jit(solution)/shard_map/ppermute | solution.py:61
  32.7 1.3 %collective-permute-start.1 = (bf16[2,112,256]{2,1,0:T(8,128)(2,1)S(1)}, bf16[2,112,256]{2,1,0:T(8,128)(2,1)S(1)}, u32[]{:S(2)}, u32[]{:S(2)}) collective-permute-start(bf16[2,112,256]{2,1,0:T(8,128)(2,1)S(1)} %broadcast_select_fusion.3), channel_id=1, source_target_pairs={{4,0},{8,4},{12,8},{5,1},{9,5},{13,9},{6,2},{10,6},{14,10},{7,3},{... | collective-permute-start | bytes 344072 | tf_op jit(solution)/shard_map/ppermute | solution.py:63
  34.0 0.0 collective-permute-done.13
  34.0 0.7 %collective-permute-start.14 = (bf16[2,112,256]{2,1,0:T(8,128)(2,1)S(1)}, bf16[2,112,256]{2,1,0:T(8,128)(2,1)S(1)}, u32[]{:S(2)}, u32[]{:S(2)}) collective-permute-start(bf16[2,112,256]{2,1,0:T(8,128)(2,1)S(1)} %collective-permute-done.13), channel_id=1, source_target_pairs={{8,12},{9,13},{10,14},{11,15},{24,28},{25,29},{26,30},{27,31}} | collective-permute-start | bytes 344072 | tf_op jit(solution)/shard_map/ppermute | solution.py:64
  34.7 0.0 collective-permute-done.4
  34.7 0.7 %collective-permute-start.5 = (bf16[2,112,256]{2,1,0:T(8,128)(2,1)S(1)}, bf16[2,112,256]{2,1,0:T(8,128)(2,1)S(1)}, u32[]{:S(2)}, u32[]{:S(2)}) collective-permute-start(bf16[2,112,256]{2,1,0:T(8,128)(2,1)S(1)} %collective-permute-done.4), channel_id=1, source_target_pairs={{8,12},{9,13},{10,14},{11,15},{24,28},{25,29},{26,30},{27,31}} | collective-permute-start | bytes 344072 | tf_op jit(solution)/shard_map/ppermute | solution.py:64
  35.4 0.3 collective-permute-done.10
  35.6 1.3 %collective-permute-start.11 = (bf16[2,112,256]{2,1,0:T(8,128)(2,1)S(1)}, bf16[2,112,256]{2,1,0:T(8,128)(2,1)S(1)}, u32[]{:S(2)}, u32[]{:S(2)}) collective-permute-start(bf16[2,112,256]{2,1,0:T(8,128)(2,1)S(1)} %collective-permute-done.10), channel_id=1, source_target_pairs={{4,0},{5,1},{6,2},{7,3},{20,16},{21,17},{22,18},{23,19}} | collective-permute-start | bytes 344072 | tf_op jit(solution)/shard_map/ppermute | solution.py:65
  36.9 2.4 %collective-permute-done.1 = bf16[2,112,256]{2,1,0:T(8,128)(2,1)S(1)} collective-permute-done((bf16[2,112,256]{2,1,0:T(8,128)(2,1)S(1)}, bf16[2,112,256]{2,1,0:T(8,128)(2,1)S(1)}, u32[]{:S(2)}, u32[]{:S(2)}) %collective-permute-start.1) | collective-permute-done | bytes 114720 | tf_op jit(solution)/shard_map/ppermute | solution.py:63
  39.4 1.3 %collective-permute-start.2 = (bf16[2,112,256]{2,1,0:T(8,128)(2,1)S(1)}, bf16[2,112,256]{2,1,0:T(8,128)(2,1)S(1)}, u32[]{:S(2)}, u32[]{:S(2)}) collective-permute-start(bf16[2,112,256]{2,1,0:T(8,128)(2,1)S(1)} %collective-permute-done.1), channel_id=1, source_target_pairs={{4,0},{5,1},{6,2},{7,3},{20,16},{21,17},{22,18},{23,19}} | collective-permute-start | bytes 344072 | tf_op jit(solution)/shard_map/ppermute | solution.py:65
  40.7 0.0 collective-permute-done.14
  40.7 0.0 collective-permute-done.5
  40.7 2.0 %collective-permute-done.11 = bf16[2,112,256]{2,1,0:T(8,128)(2,1)S(1)} collective-permute-done((bf16[2,112,256]{2,1,0:T(8,128)(2,1)S(1)}, bf16[2,112,256]{2,1,0:T(8,128)(2,1)S(1)}, u32[]{:S(2)}, u32[]{:S(2)}) %collective-permute-start.11) | collective-permute-done | bytes 114720 | tf_op jit(solution)/shard_map/ppermute | solution.py:65
  42.7 0.6 %conditional.7 = (bf16[1,2,4,64,256]{4,3,2,1,0:T(8,128)(2,1)S(1)}) conditional(s32[]{:T(128)} %clamp.4, (bf16[2,2,112,256]{3,2,1,0:T(8,128)(2,1)S(1)}, bf16[2,112,256]{2,1,0:T(8,128)(2,1)S(1)}, bf16[2,112,256]{2,1,0:T(8,128)(2,1)S(1)}, bf16[2,112,256]{2,1,0:T(8,128)(2,1)S(1)}, ...), branch_computations={%region_4.5_spmd, %region_5.6_spmd, %region_6.7_spmd, %region_7.8_... | conditional | flops 237109248 | bytes 4489224
  42.7 0.5 convolution_bitcast_fusion.4
  43.2 0.1 slice_subtract_fusion.4
  43.3 0.1 collective-permute-start.17
  43.4 1.6 %collective-permute-start.16 = (bf16[1,1,2,64,256]{4,3,2,1,0:T(8,128)(2,1)S(1)}, bf16[1,1,2,64,256]{4,3,2,1,0:T(8,128)(2,1)S(1)}, u32[]{:S(2)}, u32[]{:S(2)}) collective-permute-start(bf16[1,1,2,64,256]{4,3,2,1,0:T(8,128)(2,1)S(1)} %get-tuple-element.203), channel_id=1, source_target_pairs={{0,2},{1,3},{2,0},{3,1},{4,6},{5,7},{6,4},{7,5},{8,10},{9,11},{10,... | collective-permute-start | bytes 196616 | tf_op jit(solution)/shard_map/ppermute | solution.py:114
  45.0 0.2 collective-permute-start.15
  45.1 0.9 %collective-permute-done.2 = bf16[2,112,256]{2,1,0:T(8,128)(2,1)S(1)} collective-permute-done((bf16[2,112,256]{2,1,0:T(8,128)(2,1)S(1)}, bf16[2,112,256]{2,1,0:T(8,128)(2,1)S(1)}, u32[]{:S(2)}, u32[]{:S(2)}) %collective-permute-start.2) | collective-permute-done | bytes 114720 | tf_op jit(solution)/shard_map/ppermute | solution.py:65
  46.0 0.6 %conditional.6 = (bf16[1,2,4,64,256]{4,3,2,1,0:T(8,128)(2,1)S(1)}) conditional(s32[]{:T(128)} %clamp.4, (bf16[2,2,112,256]{3,2,0,1:T(8,128)(2,1)S(1)}, bf16[2,112,256]{2,1,0:T(8,128)(2,1)S(1)}, bf16[2,112,256]{2,1,0:T(8,128)(2,1)S(1)}, bf16[2,112,256]{2,1,0:T(8,128)(2,1)S(1)}, ...), branch_computations={%region_0.1_spmd, %region_1.2_spmd, %region_2.3_spmd, %region_3.4_... | conditional | flops 237109248 | bytes 4030472
  46.1 0.5 convolution_bitcast_fusion
  46.5 0.1 slice_subtract_fusion
  46.7 0.7 %collective-permute-start.8 = (bf16[1,1,2,64,256]{4,3,2,1,0:T(8,128)(2,1)S(1)}, bf16[1,1,2,64,256]{4,3,2,1,0:T(8,128)(2,1)S(1)}, u32[]{:S(2)}, u32[]{:S(2)}) collective-permute-start(bf16[1,1,2,64,256]{4,3,2,1,0:T(8,128)(2,1)S(1)} %get-tuple-element.199), channel_id=1, source_target_pairs={{0,3},{1,0},{2,1},{3,2},{4,7},{5,4},{6,5},{7,6},{8,11},{9,8},{10,9... | collective-permute-start | bytes 196616 | tf_op jit(solution)/shard_map/ppermute | solution.py:114
  47.4 0.9 %collective-permute-start.7 = (bf16[1,1,2,64,256]{4,3,2,1,0:T(8,128)(2,1)S(1)}, bf16[1,1,2,64,256]{4,3,2,1,0:T(8,128)(2,1)S(1)}, u32[]{:S(2)}, u32[]{:S(2)}) collective-permute-start(bf16[1,1,2,64,256]{4,3,2,1,0:T(8,128)(2,1)S(1)} %get-tuple-element.200), channel_id=1, source_target_pairs={{0,2},{1,3},{2,0},{3,1},{4,6},{5,7},{6,4},{7,5},{8,10},{9,11},{10,... | collective-permute-start | bytes 196616 | tf_op jit(solution)/shard_map/ppermute | solution.py:114
  48.3 0.9 %collective-permute-done.15 = bf16[1,1,2,64,256]{4,3,2,1,0:T(8,128)(2,1)S(1)} collective-permute-done((bf16[1,1,2,64,256]{4,3,2,1,0:T(8,128)(2,1)S(1)}, bf16[1,1,2,64,256]{4,3,2,1,0:T(8,128)(2,1)S(1)}, u32[]{:S(2)}, u32[]{:S(2)}) %collective-permute-start.15) | collective-permute-done | bytes 65568 | tf_op jit(solution)/shard_map/ppermute | solution.py:114
  49.2 0.0 collective-permute-start.6
  49.2 3.7 %collective-permute-done.6 = bf16[1,1,2,64,256]{4,3,2,1,0:T(8,128)(2,1)S(1)} collective-permute-done((bf16[1,1,2,64,256]{4,3,2,1,0:T(8,128)(2,1)S(1)}, bf16[1,1,2,64,256]{4,3,2,1,0:T(8,128)(2,1)S(1)}, u32[]{:S(2)}, u32[]{:S(2)}) %collective-permute-start.6) | collective-permute-done | bytes 65568 | tf_op jit(solution)/shard_map/ppermute | solution.py:114
  52.9 0.0 collective-permute-done.16
  53.0 0.0 collective-permute-done.7
  53.0 0.0 collective-permute-done.17
  53.0 0.0 collective-permute-done.8
  53.1 0.1 maximum_convert_fusion
  53.2 0.1 slice_bitcast_fusion.13
  53.3 4.3 %multiply_select_fusion = f32[64,32,512]{2,1,0:T(8,128)} fusion(f32[32]{0:T(128)S(1)} %get-tuple-element.210, f32[64,512]{1,0:T(8,128)S(1)} %get-tuple-element.188, f32[32]{0:T(128)S(1)} %get-tuple-element.211, f32[64,512]{1,0:T(8,128)S(1)} %get-tuple-element.189, f32[32]{0:T(128)S(1)} %get-tuple-element.212, f32[64,512]{1,0:T(8,128)S(1)} %get-tuple-element.190, ...), kind=kLoop, calls=%fused_computation.104 | loop fusion | flops 20971520 | bytes 5506048 | tf_op jit(solution)/shard_map/jit(_where)/select_n | solution.py:135
  (25 shorter events, 0.4 us)
Async XLA Ops:
  0.0 1.0 %copy-start = (bf16[1,1,2,2,112,512]{5,4,3,2,1,0:T(8,128)(2,1)S(1)}, bf16[1,1,2,2,112,512]{5,4,3,2,1,0:T(8,128)(2,1)}, u32[]{:S(2)}) copy-start(bf16[1,1,2,2,112,512]{5,4,3,2,1,0:T(8,128)(2,1)} %param.14) | copy-start | bytes 1376260
  0.0 13.6 %copy-start.2 = (s32[2,64,512]{2,1,0:T(8,128)S(1)}, s32[2,64,512]{2,1,0:T(8,128)}, u32[]{:S(2)}) copy-start(s32[2,64,512]{2,1,0:T(8,128)} %param.17) | copy-start | bytes 786436
  0.0 13.6 %copy-start.1 = (bf16[1,4,2,112,256]{4,3,2,1,0:T(8,128)(2,1)S(1)}, bf16[1,4,2,112,256]{4,3,2,1,0:T(8,128)(2,1)}, u32[]{:S(2)}) copy-start(bf16[1,4,2,112,256]{4,3,2,1,0:T(8,128)(2,1)} %param.15) | copy-start | bytes 1376260
  4.9 16.5 %collective-permute-start.3 = (bf16[2,112,256]{2,1,0:T(8,128)(2,1)S(1)}, bf16[2,112,256]{2,1,0:T(8,128)(2,1)S(1)}, u32[]{:S(2)}, u32[]{:S(2)}) collective-permute-start(bf16[2,112,256]{2,1,0:T(8,128)(2,1)S(1)} %fusion.90), channel_id=1, source_target_pairs={{0,4},{4,8},{8,12},{1,5},{5,9},{9,13},{2,6},{6,10},{10,14},{3,7},{... | collective-permute-start | bytes 344072 | tf_op jit(solution)/shard_map/ppermute | solution.py:60
  9.9 5.8 %collective-permute-start.12 = (bf16[2,112,256]{2,1,0:T(8,128)(2,1)S(1)}, bf16[2,112,256]{2,1,0:T(8,128)(2,1)S(1)}, u32[]{:S(2)}, u32[]{:S(2)}) collective-permute-start(bf16[2,112,256]{2,1,0:T(8,128)(2,1)S(1)} %fusion.86), channel_id=1, source_target_pairs={{0,4},{4,8},{8,12},{1,5},{5,9},{9,13},{2,6},{6,10},{10,14},{3,7},{... | collective-permute-start | bytes 344072 | tf_op jit(solution)/shard_map/ppermute | solution.py:60
  15.7 18.2 %collective-permute-start.13 = (bf16[2,112,256]{2,1,0:T(8,128)(2,1)S(1)}, bf16[2,112,256]{2,1,0:T(8,128)(2,1)S(1)}, u32[]{:S(2)}, u32[]{:S(2)}) collective-permute-start(bf16[2,112,256]{2,1,0:T(8,128)(2,1)S(1)} %get-tuple-element.169), channel_id=1, source_target_pairs={{0,4},{4,8},{8,12},{1,5},{5,9},{9,13},{2,6},{6,10},{10,14},{3,7},{... | collective-permute-start | bytes 344072 | tf_op jit(solution)/shard_map/ppermute | solution.py:62
  20.1 7.2 %collective-permute-start.9 = (bf16[2,112,256]{2,1,0:T(8,128)(2,1)S(1)}, bf16[2,112,256]{2,1,0:T(8,128)(2,1)S(1)}, u32[]{:S(2)}, u32[]{:S(2)}) collective-permute-start(bf16[2,112,256]{2,1,0:T(8,128)(2,1)S(1)} %get-tuple-element.170), channel_id=1, source_target_pairs={{4,0},{8,4},{12,8},{5,1},{9,5},{13,9},{6,2},{10,6},{14,10},{7,3},{... | collective-permute-start | bytes 344072 | tf_op jit(solution)/shard_map/ppermute | solution.py:61
  21.4 13.3 %collective-permute-start.4 = (bf16[2,112,256]{2,1,0:T(8,128)(2,1)S(1)}, bf16[2,112,256]{2,1,0:T(8,128)(2,1)S(1)}, u32[]{:S(2)}, u32[]{:S(2)}) collective-permute-start(bf16[2,112,256]{2,1,0:T(8,128)(2,1)S(1)} %get-tuple-element.167), channel_id=1, source_target_pairs={{0,4},{4,8},{8,12},{1,5},{5,9},{9,13},{2,6},{6,10},{10,14},{3,7},{... | collective-permute-start | bytes 344072 | tf_op jit(solution)/shard_map/ppermute | solution.py:62
  26.0 6.7 %collective-permute-start = (bf16[2,112,256]{2,1,0:T(8,128)(2,1)S(1)}, bf16[2,112,256]{2,1,0:T(8,128)(2,1)S(1)}, u32[]{:S(2)}, u32[]{:S(2)}) collective-permute-start(bf16[2,112,256]{2,1,0:T(8,128)(2,1)S(1)} %get-tuple-element.168), channel_id=1, source_target_pairs={{4,0},{8,4},{12,8},{5,1},{9,5},{13,9},{6,2},{10,6},{14,10},{7,3},{... | collective-permute-start | bytes 344072 | tf_op jit(solution)/shard_map/ppermute | solution.py:61
  27.3 8.3 %collective-permute-start.10 = (bf16[2,112,256]{2,1,0:T(8,128)(2,1)S(1)}, bf16[2,112,256]{2,1,0:T(8,128)(2,1)S(1)}, u32[]{:S(2)}, u32[]{:S(2)}) collective-permute-start(bf16[2,112,256]{2,1,0:T(8,128)(2,1)S(1)} %broadcast_select_fusion.2), channel_id=1, source_target_pairs={{4,0},{8,4},{12,8},{5,1},{9,5},{13,9},{6,2},{10,6},{14,10},{7,3},{... | collective-permute-start | bytes 344072 | tf_op jit(solution)/shard_map/ppermute | solution.py:63
  32.7 6.7 %collective-permute-start.1 = (bf16[2,112,256]{2,1,0:T(8,128)(2,1)S(1)}, bf16[2,112,256]{2,1,0:T(8,128)(2,1)S(1)}, u32[]{:S(2)}, u32[]{:S(2)}) collective-permute-start(bf16[2,112,256]{2,1,0:T(8,128)(2,1)S(1)} %broadcast_select_fusion.3), channel_id=1, source_target_pairs={{4,0},{8,4},{12,8},{5,1},{9,5},{13,9},{6,2},{10,6},{14,10},{7,3},{... | collective-permute-start | bytes 344072 | tf_op jit(solution)/shard_map/ppermute | solution.py:63
  34.0 6.7 %collective-permute-start.14 = (bf16[2,112,256]{2,1,0:T(8,128)(2,1)S(1)}, bf16[2,112,256]{2,1,0:T(8,128)(2,1)S(1)}, u32[]{:S(2)}, u32[]{:S(2)}) collective-permute-start(bf16[2,112,256]{2,1,0:T(8,128)(2,1)S(1)} %collective-permute-done.13), channel_id=1, source_target_pairs={{8,12},{9,13},{10,14},{11,15},{24,28},{25,29},{26,30},{27,31}} | collective-permute-start | bytes 344072 | tf_op jit(solution)/shard_map/ppermute | solution.py:64
  34.7 6.0 %collective-permute-start.5 = (bf16[2,112,256]{2,1,0:T(8,128)(2,1)S(1)}, bf16[2,112,256]{2,1,0:T(8,128)(2,1)S(1)}, u32[]{:S(2)}, u32[]{:S(2)}) collective-permute-start(bf16[2,112,256]{2,1,0:T(8,128)(2,1)S(1)} %collective-permute-done.4), channel_id=1, source_target_pairs={{8,12},{9,13},{10,14},{11,15},{24,28},{25,29},{26,30},{27,31}} | collective-permute-start | bytes 344072 | tf_op jit(solution)/shard_map/ppermute | solution.py:64
  35.6 7.0 %collective-permute-start.11 = (bf16[2,112,256]{2,1,0:T(8,128)(2,1)S(1)}, bf16[2,112,256]{2,1,0:T(8,128)(2,1)S(1)}, u32[]{:S(2)}, u32[]{:S(2)}) collective-permute-start(bf16[2,112,256]{2,1,0:T(8,128)(2,1)S(1)} %collective-permute-done.10), channel_id=1, source_target_pairs={{4,0},{5,1},{6,2},{7,3},{20,16},{21,17},{22,18},{23,19}} | collective-permute-start | bytes 344072 | tf_op jit(solution)/shard_map/ppermute | solution.py:65
  39.4 6.7 %collective-permute-start.2 = (bf16[2,112,256]{2,1,0:T(8,128)(2,1)S(1)}, bf16[2,112,256]{2,1,0:T(8,128)(2,1)S(1)}, u32[]{:S(2)}, u32[]{:S(2)}) collective-permute-start(bf16[2,112,256]{2,1,0:T(8,128)(2,1)S(1)} %collective-permute-done.1), channel_id=1, source_target_pairs={{4,0},{5,1},{6,2},{7,3},{20,16},{21,17},{22,18},{23,19}} | collective-permute-start | bytes 344072 | tf_op jit(solution)/shard_map/ppermute | solution.py:65
  43.3 9.7 %collective-permute-start.17 = (bf16[1,1,2,64,256]{4,3,2,1,0:T(8,128)(2,1)S(1)}, bf16[1,1,2,64,256]{4,3,2,1,0:T(8,128)(2,1)S(1)}, u32[]{:S(2)}, u32[]{:S(2)}) collective-permute-start(bf16[1,1,2,64,256]{4,3,2,1,0:T(8,128)(2,1)S(1)} %get-tuple-element.202), channel_id=1, source_target_pairs={{0,3},{1,0},{2,1},{3,2},{4,7},{5,4},{6,5},{7,6},{8,11},{9,8},{10,9... | collective-permute-start | bytes 196616 | tf_op jit(solution)/shard_map/ppermute | solution.py:114
  43.4 9.5 %collective-permute-start.16 = (bf16[1,1,2,64,256]{4,3,2,1,0:T(8,128)(2,1)S(1)}, bf16[1,1,2,64,256]{4,3,2,1,0:T(8,128)(2,1)S(1)}, u32[]{:S(2)}, u32[]{:S(2)}) collective-permute-start(bf16[1,1,2,64,256]{4,3,2,1,0:T(8,128)(2,1)S(1)} %get-tuple-element.203), channel_id=1, source_target_pairs={{0,2},{1,3},{2,0},{3,1},{4,6},{5,7},{6,4},{7,5},{8,10},{9,11},{10,... | collective-permute-start | bytes 196616 | tf_op jit(solution)/shard_map/ppermute | solution.py:114
  45.0 4.3 %collective-permute-start.15 = (bf16[1,1,2,64,256]{4,3,2,1,0:T(8,128)(2,1)S(1)}, bf16[1,1,2,64,256]{4,3,2,1,0:T(8,128)(2,1)S(1)}, u32[]{:S(2)}, u32[]{:S(2)}) collective-permute-start(bf16[1,1,2,64,256]{4,3,2,1,0:T(8,128)(2,1)S(1)} %get-tuple-element.204), channel_id=1, source_target_pairs={{0,1},{1,2},{2,3},{3,0},{4,5},{5,6},{6,7},{7,4},{8,9},{9,10},{10,1... | collective-permute-start | bytes 196616 | tf_op jit(solution)/shard_map/ppermute | solution.py:114
  46.7 6.3 %collective-permute-start.8 = (bf16[1,1,2,64,256]{4,3,2,1,0:T(8,128)(2,1)S(1)}, bf16[1,1,2,64,256]{4,3,2,1,0:T(8,128)(2,1)S(1)}, u32[]{:S(2)}, u32[]{:S(2)}) collective-permute-start(bf16[1,1,2,64,256]{4,3,2,1,0:T(8,128)(2,1)S(1)} %get-tuple-element.199), channel_id=1, source_target_pairs={{0,3},{1,0},{2,1},{3,2},{4,7},{5,4},{6,5},{7,6},{8,11},{9,8},{10,9... | collective-permute-start | bytes 196616 | tf_op jit(solution)/shard_map/ppermute | solution.py:114
  47.4 5.6 %collective-permute-start.7 = (bf16[1,1,2,64,256]{4,3,2,1,0:T(8,128)(2,1)S(1)}, bf16[1,1,2,64,256]{4,3,2,1,0:T(8,128)(2,1)S(1)}, u32[]{:S(2)}, u32[]{:S(2)}) collective-permute-start(bf16[1,1,2,64,256]{4,3,2,1,0:T(8,128)(2,1)S(1)} %get-tuple-element.200), channel_id=1, source_target_pairs={{0,2},{1,3},{2,0},{3,1},{4,6},{5,7},{6,4},{7,5},{8,10},{9,11},{10,... | collective-permute-start | bytes 196616 | tf_op jit(solution)/shard_map/ppermute | solution.py:114
  49.2 3.7 %collective-permute-start.6 = (bf16[1,1,2,64,256]{4,3,2,1,0:T(8,128)(2,1)S(1)}, bf16[1,1,2,64,256]{4,3,2,1,0:T(8,128)(2,1)S(1)}, u32[]{:S(2)}, u32[]{:S(2)}) collective-permute-start(bf16[1,1,2,64,256]{4,3,2,1,0:T(8,128)(2,1)S(1)} %get-tuple-element.201), channel_id=1, source_target_pairs={{0,1},{1,2},{2,3},{3,0},{4,5},{5,6},{6,7},{7,4},{8,9},{9,10},{10,1... | collective-permute-start | bytes 196616 | tf_op jit(solution)/shard_map/ppermute | solution.py:114
